TPU v7x, 256 devices: a whole 4x4x8 slice. The times are simulated.
256 devices in a mesh: row: 8 (over y, core), col: 16 (over x_lo, z), req: 2 (over x_hi).
Axes of the slice: x: 4 (x_hi: 2, x_lo: 2; x = x_hi * 2 + x_lo), y: 4, z: 8, core: 2. Of those that a mesh axis runs over, the one named last changes fastest.
Arguments:
- tokens: bfloat16 [3072, 4096], P(('req', 'row'), 'col'), may hold values from -6 to 6
- up_weight: bfloat16 [4096, 21504], P('col', 'row'), may hold values from -0.09375 to 0.09375
- down_weight: bfloat16 [21504, 4096], P('row', 'col'), may hold values from -0.0390625 to 0.0390625
- pool_states: float32 [192, 2, 128, 64, 128], P('row', 'req', 'col'), may hold values from -6 to 6
- pool_edges: float32 [192, 2, 128, 64, 3], P('row', 'req', 'col'), may hold values from -6 to 6
- finish_ids: int32 [32], replicated, may hold values from 0 to 191, as said below
- slot_perm: int32 [32], replicated, may hold values from 0 to 31, each once
Outputs:
- layer_out: bfloat16 [3072, 4096], P(('req', 'row'), 'col')
- decode_states: float32 [32, 2, 128, 64, 128], P('req', None, 'col', 'row')
- decode_edges: float32 [32, 2, 128, 64, 3], P('req', None, 'col', 'row')
Inputs may be any that keep to these rules, and one draw needn't show every extreme that they name: `finish_ids`: entries are distinct; of the 24 slots r * 24 to (r + 1) * 24 - 1 of one index r of row, at most 8 are named, and exactly 8 for some index. `slot_perm`: every decode slot is named once.
All inputs are finite; a program needn't handle non-finite values.
Results may differ from a plain program's by a relative error of at most 0.0044.
Values may be sent and summed in bfloat16 or wider, within the bound.
No kernel may reach another device: no remote copies, remote signals or barrier semaphores. Data moves between devices by JAX's collectives and lax.ppermute only.
A program may use at most 128 MiB of HBM per device.

v0:
```python
import jax
import jax.numpy as jnp
import numpy as np
from jax import lax
from jax.sharding import Mesh
from jax.sharding import PartitionSpec as P

MOST = 8
SWAP = [(0, 1), (1, 0)]


def handover(pool_states, pool_edges, finish_ids, slot_perm):
    local = pool_states.shape[0]
    finished = slot_perm.shape[0]
    r = lax.axis_index("row")
    numbers = jnp.arange(finished, dtype=jnp.int32)
    matches = slot_perm[None, :] == numbers[:, None]
    inverse = jnp.sum(jnp.where(matches, numbers[None, :], 0), axis=1)
    row_of = finish_ids // local
    same = row_of[:, None] == row_of[None, :]
    earlier = numbers[None, :] < numbers[:, None]
    rank = jnp.sum(jnp.where(same & earlier, 1, 0), axis=1)
    slots = jnp.arange(MOST, dtype=jnp.int32)
    chosen = (row_of[None, :] == r) & (rank[None, :] == slots[:, None])
    local_slot = jnp.sum(jnp.where(chosen, finish_ids[None, :] - r * local, 0), axis=1)
    picked = jnp.concatenate([pool_states[local_slot], pool_edges[local_slot]], axis=-1)
    arrived = lax.all_to_all(picked, "row", split_axis=3, concat_axis=0, tiled=True)
    source = inverse
    wanted = row_of[source] * MOST + rank[source]
    rows = arrived[wanted]
    both = lax.all_to_all(rows, "req", split_axis=0, concat_axis=1, tiled=True)
    n = pool_states.shape[-1]
    return (both[..., :n], both[..., n:])


def ffn(tokens, up_weight, down_weight):
    i = lax.axis_index("cx")
    block, width = tokens.shape
    half = block // 2
    halves = tokens.reshape(2, half, width)
    mine = lax.dynamic_index_in_dim(halves, i, 0, keepdims=False)
    theirs = lax.dynamic_index_in_dim(halves, 1 - i, 0, keepdims=False)
    recv = lax.ppermute(theirs, "cx", SWAP)
    xa = jnp.concatenate([mine, recv], axis=1)
    xg = lax.all_gather(xa, "row", axis=0, tiled=True)
    w1 = jnp.concatenate([up_weight, lax.ppermute(up_weight, "cx", SWAP)], axis=0)
    preact = lax.psum_scatter(
        jnp.dot(xg, w1, preferred_element_type=jnp.float32), "cz", scatter_dimension=0, tiled=True
    )
    active = jnp.maximum(preact, 0.0)
    hidden = (active * active).astype(jnp.bfloat16)
    hg = lax.all_gather(hidden, "cz", axis=0, tiled=True)
    w2 = jnp.concatenate([down_weight, lax.ppermute(down_weight, "cx", SWAP)], axis=1)
    products = jnp.dot(hg, w2, preferred_element_type=jnp.float32)
    summed = lax.psum_scatter(products, "row", scatter_dimension=0, tiled=True)
    own = summed[:, :width]
    other = lax.ppermute(summed[:, width:], "cx", SWAP)
    full = jnp.where(i == 0, jnp.concatenate([own, other], 0), jnp.concatenate([other, own], 0))
    return (tokens.astype(jnp.float32) + full).astype(jnp.bfloat16)


def on_device(tokens, up_weight, down_weight, pool_states, pool_edges, finish_ids, slot_perm):
    layer_out = ffn(tokens, up_weight, down_weight)
    decode_states, decode_edges = handover(pool_states, pool_edges, finish_ids, slot_perm)
    return (layer_out, decode_states, decode_edges)


def solution(mesh):
    devices = np.asarray(mesh.devices)
    rows, cols, reqs = devices.shape
    split = Mesh(devices.reshape(rows, 2, cols // 2, reqs), ("row", "cx", "cz", "req"))
    col = ("cx", "cz")
    in_specs = (
        P(("req", "row"), col),
        P(col, "row"),
        P("row", col),
        P("row", "req", col, None, None),
        P("row", "req", col, None, None),
        P(),
        P(),
    )
    out_specs = (
        P(("req", "row"), col),
        P("req", None, col, "row", None),
        P("req", None, col, "row", None),
    )
    return jax.shard_map(
        on_device, mesh=split, in_specs=in_specs, out_specs=out_specs, check_vma=False
    )
```

profile of v0, /device:TPU:2, one launch (start us, length us, event | category | flops | bytes accessed | tf_op | source)
XLA Modules:
  0.0 343.2 jit_solution(12249648840841902804)
XLA Ops:
  7.2 2.3 collective-permute-start.1
  10.5 30.0 %collective-permute-done = bf16[96,256]{1,0:T(8,128)(2,1)S(1)} collective-permute-done((bf16[96,256]{1,0:T(8,128)(2,1)S(1)}, bf16[96,256]{1,0:T(8,128)(2,1)S(1)}, u32[]{:S(2)}, u32[]{:S(2)}) %collective-permute-start) | collective-permute-done | bytes 49184 | tf_op jit(solution)/shard_map/ppermute | solution.py:43
  40.5 13.9 %all_gather.6 = bf16[768,512]{1,0:T(8,128)(2,1)S(1)} all-gather(bf16[96,512]{1,0:T(8,128)(2,1)S(1)} %pad_maximum_fusion.1), channel_id=1, replica_groups=mesh['row'=8,'cx'=2,'cz'=8,'req'=2] {'row'}, dimensions={0}, use_global_device_ids=true | all-gather | bytes 884736 | tf_op jit(solution)/shard_map/all_gather | solution.py:45
  54.4 6.9 %fusion = f32[768,2688]{1,0:T(8,128)} fusion(bf16[768,512]{1,0:T(8,128)(2,1)S(1)} %all_gather.6, bf16[256,2688]{1,0:T(8,128)(2,1)S(1)} %collective-permute-done.1, bf16[256,2688]{1,0:T(8,128)(2,1)} %param.8), kind=kOutput, calls=%fused_computation.7 | convolution fusion | flops 2119434240 | bytes 11796480 | tf_op jit(solution)/shard_map/dot_general | solution.py:48
  61.4 96.0 %reduce-scatter.3.cloned.1.call-done = f32[96,2688]{1,0:T(8,128)} async-done(((f32[768,2688]{1,0:T(8,128)}), f32[96,2688]{1,0:T(8,128)}) %reduce-scatter.3.cloned.1.call-update) | async-done | bytes 1032208 | tf_op jit(solution)/shard_map/reduce_scatter | solution.py:47
  157.5 2.1 multiply_convert_fusion
  160.3 31.3 %collective-permute-done.2 = bf16[2688,256]{1,0:T(8,128)(2,1)S(1)} collective-permute-done((bf16[2688,256]{1,0:T(8,128)(2,1)S(1)}, bf16[2688,256]{1,0:T(8,128)(2,1)S(1)}, u32[]{:S(2)}, u32[]{:S(2)}) %collective-permute-start.2) | collective-permute-done | bytes 1376288 | tf_op jit(solution)/shard_map/ppermute | solution.py:53
  191.6 21.0 %all-gather.2.cloned.1.call-done = bf16[768,2688]{1,0:T(8,128)(2,1)} async-done(((bf16[96,2688]{1,0:T(8,128)(2,1)}), bf16[768,2688]{1,0:T(8,128)(2,1)}) %all-gather.2.cloned.1.call-update) | async-done | bytes 4128784 | tf_op jit(solution)/shard_map/all_gather | solution.py:52
  212.7 5.7 %fusion.4 = f32[768,512]{1,0:T(8,128)} fusion(bf16[768,2688]{1,0:T(8,128)(2,1)} %all-gather.2.cloned.1.call-done, bf16[2688,256]{1,0:T(8,128)(2,1)S(1)} %collective-permute-done.2, bf16[2688,256]{1,0:T(8,128)(2,1)S(1)} %copy-done.4), kind=kOutput, calls=%fused_computation.11 | convolution fusion | flops 2119434240 | bytes 8454144 | tf_op jit(solution)/shard_map/dot_general | solution.py:54
  220.1 4.8 %gather_fusion = f32[8,8,64,128]{3,2,1,0:T(8,128)} fusion(f32[24,8,64,128]{3,2,1,0:T(8,128)} %bitcast.45, s32[1024]{0:T(1024)S(1)} %pad_clamp_fusion.2), kind=kCustom, calls=%fused_computation | custom fusion | bytes 4194336 | tf_op jit(solution)/shard_map/gather | solution.py:26
  224.9 2.0 pad_maximum_fusion
  226.9 4.4 %copy.36 = f32[8,1,8,64,131]{4,2,0,1,3:T(8,128)} copy(f32[8,1,8,64,131]{4,3,2,0,1:T(8,128)S(1)} %pad_maximum_fusion) | data formatting | bytes 4292608 | tf_op jit(solution)/shard_map/concatenate | solution.py:26
  231.3 4.9 %all-to-all-start = ((f32[8,1,8,64,131]{4,2,0,1,3:T(8,128)}), f32[8,1,8,64,131]{4,2,0,1,3:T(8,128)}, u32[]{:S(2)}, u32[]{:S(2)}) async-start(f32[8,1,8,64,131]{4,2,0,1,3:T(8,128)} %copy.36), calls=%async_computation.2 | async-start | bytes 8388608 | tf_op jit(solution)/shard_map/all_to_all | solution.py:27
  237.8 51.6 %all-to-all-done = f32[8,1,8,64,131]{4,2,0,1,3:T(8,128)} async-done(((f32[8,1,8,64,131]{4,2,0,1,3:T(8,128)}), f32[8,1,8,64,131]{4,2,0,1,3:T(8,128)}, u32[]{:S(2)}, u32[]{:S(2)}) %all-to-all-start) | async-done | bytes 2146336 | tf_op jit(solution)/shard_map/all_to_all | solution.py:27
  289.4 4.6 %copy.43 = f32[8,1,8,64,131]{4,3,2,0,1:T(8,128)S(1)} copy(f32[8,1,8,64,131]{4,2,0,1,3:T(8,128)} %all-to-all-done) | data formatting | bytes 4292608 | tf_op jit(solution)/shard_map/all_to_all | solution.py:27
  294.0 2.6 copy.38
  296.6 4.2 %gather_fusion.4 = f32[32,8,8,131]{3,2,1,0:T(8,128)} fusion(f32[64,8,8,131]{3,2,1,0:T(8,128)} %bitcast.39, s32[1024]{0:T(1024)S(1)} %pad_clamp_fusion), kind=kCustom, calls=%fused_computation.4 | custom fusion | bytes 2146432 | tf_op jit(solution)/shard_map/gather | solution.py:30
  300.7 3.8 %all-to-all-start.1 = ((f32[32,1,8,8,131]{4,3,2,1,0:T(8,128)}), f32[32,1,8,8,131]{4,3,2,1,0:T(8,128)S(1)}, u32[]{:S(2)}, u32[]{:S(2)}) async-start(f32[32,1,8,8,131]{4,3,2,1,0:T(8,128)} %bitcast.42), calls=%async_computation.3 | async-start | bytes 4194304 | tf_op jit(solution)/shard_map/all_to_all | solution.py:31
  304.5 1.6 fusion.17
  306.2 1.0 collective-permute-start.3
  307.2 25.0 %all-to-all-done.1 = f32[32,1,8,8,131]{4,3,2,1,0:T(8,128)S(1)} async-done(((f32[32,1,8,8,131]{4,3,2,1,0:T(8,128)}), f32[32,1,8,8,131]{4,3,2,1,0:T(8,128)S(1)}, u32[]{:S(2)}, u32[]{:S(2)}) %all-to-all-start.1) | async-done | bytes 1073184 | tf_op jit(solution)/shard_map/all_to_all | solution.py:31
  332.3 1.1 copy.40
  333.4 1.5 copy.41
  335.0 1.6 fusion.9
  (42 shorter events, 5.1 us)
Async XLA Ops:
  7.2 211.6 %copy-start = (f32[24,1,8,64,3]{3,2,4,1,0:T(8,128)S(1)}, f32[24,1,8,64,3]{3,2,4,1,0:T(8,128)}, u32[]{:S(2)}) copy-start(f32[24,1,8,64,3]{3,2,4,1,0:T(8,128)} %param.11) | copy-start | bytes 442372
  7.2 150.3 %reduce-scatter.3.cloned.1.call-start = ((), (), s32[]{:S(2)}) async-start(), calls=%async_computation.4 | async-start | bytes 9289728 | tf_op jit(solution)/shard_map/reduce_scatter | solution.py:47
  7.2 47.2 %collective-permute-start.1 = (bf16[256,2688]{1,0:T(8,128)(2,1)}, bf16[256,2688]{1,0:T(8,128)(2,1)S(1)}, u32[]{:S(2)}, u32[]{:S(2)}) collective-permute-start(bf16[256,2688]{1,0:T(8,128)(2,1)} %param.8), channel_id=1, source_target_pairs={{0,16},{16,0},{1,17},{17,1},{2,18},{18,2},{3,19},{19,3},{4,20},{20... | collective-permute-start | bytes 4128776 | tf_op jit(solution)/shard_map/ppermute | solution.py:46
  10.4 30.1 %collective-permute-start = (bf16[96,256]{1,0:T(8,128)(2,1)S(1)}, bf16[96,256]{1,0:T(8,128)(2,1)S(1)}, u32[]{:S(2)}, u32[]{:S(2)}) collective-permute-start(bf16[96,256]{1,0:T(8,128)(2,1)S(1)} %get-tuple-element.29), channel_id=1, source_target_pairs={{0,16},{16,0},{1,17},{17,1},{2,18},{18,2},{3,19},{19,3},{4,20},{20... | collective-permute-start | bytes 147464 | tf_op jit(solution)/shard_map/ppermute | solution.py:43
  61.4 98.3 %copy-start.4 = (bf16[2688,256]{1,0:T(8,128)(2,1)S(1)}, bf16[2688,256]{1,0:T(8,128)(2,1)}, u32[]{:S(2)}) copy-start(bf16[2688,256]{1,0:T(8,128)(2,1)} %param.9) | copy-start | bytes 4128772
  61.4 151.3 %all-gather.2.cloned.1.call-start = ((), (), s32[]{:S(2)}) async-start(), calls=%async_computation.5 | async-start | bytes 4644864 | tf_op jit(solution)/shard_map/all_gather | solution.py:52
  159.6 144.9 %reduce-scatter.5.cloned.1.call-start = ((), (), s32[]{:S(2)}) async-start(), calls=%async_computation.6 | async-start | bytes 1769472 | tf_op jit(solution)/shard_map/reduce_scatter | solution.py:55
  159.6 32.0 %collective-permute-start.2 = (bf16[2688,256]{1,0:T(8,128)(2,1)S(1)}, bf16[2688,256]{1,0:T(8,128)(2,1)S(1)}, u32[]{:S(2)}, u32[]{:S(2)}) collective-permute-start(bf16[2688,256]{1,0:T(8,128)(2,1)S(1)} %copy-done.4), channel_id=1, source_target_pairs={{0,16},{16,0},{1,17},{17,1},{2,18},{18,2},{3,19},{19,3},{4,20},{20... | collective-permute-start | bytes 4128776 | tf_op jit(solution)/shard_map/ppermute | solution.py:53
  160.3 58.1 %copy-start.3 = (s32[32]{0:T(128)S(1)}, s32[32]{0:T(128)}, u32[]{:S(2)}) copy-start(s32[32]{0:T(128)} %param.12) | copy-start | bytes 388
  231.3 4.9 %copy-start.5 = (s32[32]{0:T(128)S(1)}, s32[32]{0:T(128)}, u32[]{:S(2)}) copy-start(s32[32]{0:T(128)} %param.13) | copy-start | bytes 388
  231.3 58.0 %all-to-all-start = ((f32[8,1,8,64,131]{4,2,0,1,3:T(8,128)}), f32[8,1,8,64,131]{4,2,0,1,3:T(8,128)}, u32[]{:S(2)}, u32[]{:S(2)}) async-start(f32[8,1,8,64,131]{4,2,0,1,3:T(8,128)} %copy.36), calls=%async_computation.2 | async-start | bytes 8388608 | tf_op jit(solution)/shard_map/all_to_all | solution.py:27
  300.7 31.4 %all-to-all-start.1 = ((f32[32,1,8,8,131]{4,3,2,1,0:T(8,128)}), f32[32,1,8,8,131]{4,3,2,1,0:T(8,128)S(1)}, u32[]{:S(2)}, u32[]{:S(2)}) async-start(f32[32,1,8,8,131]{4,3,2,1,0:T(8,128)} %bitcast.42), calls=%async_computation.3 | async-start | bytes 4194304 | tf_op jit(solution)/shard_map/all_to_all | solution.py:31
  306.2 28.8 %collective-permute-start.3 = (f32[96,256]{1,0:T(8,128)}, f32[96,256]{1,0:T(8,128)}, u32[]{:S(2)}, u32[]{:S(2)}) collective-permute-start(f32[96,256]{1,0:T(8,128)} %get-tuple-element.27), channel_id=1, source_target_pairs={{0,16},{16,0},{1,17},{17,1},{2,18},{18,2},{3,19},{19,3},{4,20},{20... | collective-permute-start | bytes 294920 | tf_op jit(solution)/shard_map/ppermute | solution.py:57
  332.2 2.8 copy-start.1
  332.3 2.7 copy-start.2
Sparse Core Ops, SparseCore 0:
  61.5 95.9 reduce-scatter.2
  159.8 52.7 all-gather.1
  218.5 41.6 reduce-scatter.4
where the time goes:
time: 344 us; the launch traced here: 343 us
  waiting for transfers between devices  255 us (74%)
  local copies, waits for them, and re-layouts  28.5 us (8%)
  blocking collectives  13.9 us (4%)
  between operations  13.9 us (4%)
  starting transfers between devices  12.8 us (4%)
  matrix products  12.7 us (4%)
  other arithmetic  6.26 us (2%)
    reduce_scatter x1, waiting for transfers between devices, ffn(): lax.psum_scatter(jnp.dot(xg, w1, preferred_element_type=jnp.float32), 'cz...  96 us
    all_to_all x1, waiting for transfers between devices, handover(): lax.all_to_all(picked, 'row', split_axis=3, concat_axis=0, tiled=True)  51.6 us
    ppermute x1, waiting for transfers between devices, ffn(): lax.ppermute(down_weight, 'cx', SWAP)  31.3 us
    ppermute x1, waiting for transfers between devices, ffn(): recv = lax.ppermute(theirs, 'cx', SWAP)  30 us
    all_to_all x1, waiting for transfers between devices, handover(): both = lax.all_to_all(rows, 'req', split_axis=0, concat_axis=1, tiled=True)  25 us
    all_gather x1, waiting for transfers between devices, ffn(): hg = lax.all_gather(hidden, 'cz', axis=0, tiled=True)  21 us
    all_gather x1, blocking collectives, ffn(): xg = lax.all_gather(xa, 'row', axis=0, tiled=True)  13.9 us
    all_to_all x2, local copies, waits for them, and re-layouts, handover(): lax.all_to_all(picked, 'row', split_axis=3, concat_axis=0, tiled=True)  7.19 us
  transfers between devices with their start and end apart: 9, of which 6 were waited for; matrix products, arithmetic and copies ran while one was open for 9% of the time, Pallas kernels for 0%

commit v1 on v0

--- a/solution.py
+++ b/solution.py
@@ -49,7 +49,9 @@
     )
     active = jnp.maximum(preact, 0.0)
     hidden = (active * active).astype(jnp.bfloat16)
-    hg = lax.all_gather(hidden, "cz", axis=0, tiled=True)
+    hg = jnp.concatenate(
+        lax.all_to_all(jnp.stack([hidden] * lax.axis_size("cz")), "cz", 0, 0), axis=0
+    )
     w2 = jnp.concatenate([down_weight, lax.ppermute(down_weight, "cx", SWAP)], axis=1)
     products = jnp.dot(hg, w2, preferred_element_type=jnp.float32)
     summed = lax.psum_scatter(products, "row", scatter_dimension=0, tiled=True)

time: 344 us -> 391 us (1.14)
  waiting for transfers between devices: 255 us -> 296 us
  starting transfers between devices: 12.8 us -> 17.5 us
    all_to_all x0 -> x1, waiting for transfers between devices: none -> 63 us  [ffn(): lax.all_to_all(jnp.stack([hidden] * lax.axis_size('cz')), 'cz', 0, 0)]
    all_gather x1 -> x0, waiting for transfers between devices: 21 us -> none  [ffn(): hg = lax.all_gather(hidden, 'cz', axis=0, tiled=True)]
    all_to_all x0 -> x1, starting transfers between devices: none -> 4.67 us  [ffn(): lax.all_to_all(jnp.stack([hidden] * lax.axis_size('cz')), 'cz', 0, 0)]
  transfers between devices with their start and end apart: 9 -> 9, of which waited for: 6 -> 6; matrix products, arithmetic and copies ran while one was open for 9% -> 8% of each run, Pallas kernels for 0% -> 0%
where the time goes in v1:
time: 391 us
  waiting for transfers between devices  296 us (76%)
  local copies, waits for them, and re-layouts  30.8 us (8%)
  starting transfers between devices  17.5 us (4%)
  between operations  14.2 us (4%)
  blocking collectives  13.9 us (4%)
  matrix products  12.7 us (3%)
  other arithmetic  5.58 us (1%)
    reduce_scatter x1, waiting for transfers between devices, ffn(): lax.psum_scatter(jnp.dot(xg, w1, preferred_element_type=jnp.float32), 'cz...  96.1 us
    all_to_all x1, waiting for transfers between devices, ffn(): lax.all_to_all(jnp.stack([hidden] * lax.axis_size('cz')), 'cz', 0, 0)  63 us
    all_to_all x1, waiting for transfers between devices, handover(): lax.all_to_all(picked, 'row', split_axis=3, concat_axis=0, tiled=True)  50.8 us
    ppermute x1, waiting for transfers between devices, ffn(): lax.ppermute(down_weight, 'cx', SWAP)  31.3 us
    ppermute x1, waiting for transfers between devices, ffn(): recv = lax.ppermute(theirs, 'cx', SWAP)  30 us
    all_to_all x1, waiting for transfers between devices, handover(): both = lax.all_to_all(rows, 'req', split_axis=0, concat_axis=1, tiled=True)  24.8 us
    all_gather x1, blocking collectives, ffn(): xg = lax.all_gather(xa, 'row', axis=0, tiled=True)  13.9 us
  transfers between devices with their start and end apart: 9, of which 6 were waited for; matrix products, arithmetic and copies ran while one was open for 8% of the time, Pallas kernels for 0%

profile of v1, /device:TPU:2, one launch (start us, length us, event | category | flops | bytes accessed | tf_op | source)
XLA Modules:
  0.0 390.7 jit_solution(1998561989503055132)
XLA Ops:
  7.2 2.3 collective-permute-start.1
  10.5 30.0 %collective-permute-done = bf16[96,256]{1,0:T(8,128)(2,1)S(1)} collective-permute-done((bf16[96,256]{1,0:T(8,128)(2,1)S(1)}, bf16[96,256]{1,0:T(8,128)(2,1)S(1)}, u32[]{:S(2)}, u32[]{:S(2)}) %collective-permute-start) | collective-permute-done | bytes 49184 | tf_op jit(solution)/shard_map/ppermute | solution.py:43
  40.5 13.9 %all_gather.3 = bf16[768,512]{1,0:T(8,128)(2,1)S(1)} all-gather(bf16[96,512]{1,0:T(8,128)(2,1)S(1)} %pad_maximum_fusion.1), channel_id=1, replica_groups=mesh['row'=8,'cx'=2,'cz'=8,'req'=2] {'row'}, dimensions={0}, use_global_device_ids=true | all-gather | bytes 884736 | tf_op jit(solution)/shard_map/all_gather | solution.py:45
  54.4 6.9 %fusion = f32[768,2688]{1,0:T(8,128)} fusion(bf16[768,512]{1,0:T(8,128)(2,1)S(1)} %all_gather.3, bf16[256,2688]{1,0:T(8,128)(2,1)S(1)} %collective-permute-done.1, bf16[256,2688]{1,0:T(8,128)(2,1)} %param.8), kind=kOutput, calls=%fused_computation.7 | convolution fusion | flops 2119434240 | bytes 11796480 | tf_op jit(solution)/shard_map/dot_general | solution.py:48
  61.4 96.1 %reduce-scatter.3.cloned.1.call-done = f32[96,2688]{1,0:T(8,128)} async-done(((f32[768,2688]{1,0:T(8,128)}), f32[96,2688]{1,0:T(8,128)}) %reduce-scatter.3.cloned.1.call-update) | async-done | bytes 1032208 | tf_op jit(solution)/shard_map/reduce_scatter | solution.py:47
  157.5 1.3 multiply_convert_fusion
  158.8 2.2 stack.2
  161.0 4.7 %all-to-all-start = ((bf16[8,96,2688]{2,1,0:T(8,128)(2,1)}), bf16[8,96,2688]{2,1,0:T(8,128)(2,1)}, u32[]{:S(2)}, u32[]{:S(2)}) async-start(bf16[8,96,2688]{2,1,0:T(8,128)(2,1)} %stack.2), calls=%async_computation.1 | async-start | bytes 8257536 | tf_op jit(solution)/shard_map/all_to_all | solution.py:53
  166.4 31.3 %collective-permute-done.2 = bf16[2688,256]{1,0:T(8,128)(2,1)S(1)} collective-permute-done((bf16[2688,256]{1,0:T(8,128)(2,1)S(1)}, bf16[2688,256]{1,0:T(8,128)(2,1)S(1)}, u32[]{:S(2)}, u32[]{:S(2)}) %collective-permute-start.2) | collective-permute-done | bytes 1376288 | tf_op jit(solution)/shard_map/ppermute | solution.py:55
  197.7 63.0 %all-to-all-done = bf16[8,96,2688]{2,1,0:T(8,128)(2,1)} async-done(((bf16[8,96,2688]{2,1,0:T(8,128)(2,1)}), bf16[8,96,2688]{2,1,0:T(8,128)(2,1)}, u32[]{:S(2)}, u32[]{:S(2)}) %all-to-all-start) | async-done | bytes 4128800 | tf_op jit(solution)/shard_map/all_to_all | solution.py:53
  260.8 5.8 %fusion.4 = f32[768,512]{1,0:T(8,128)} fusion(bf16[768,2688]{1,0:T(8,128)(2,1)} %bitcast.3, bf16[2688,256]{1,0:T(8,128)(2,1)S(1)} %collective-permute-done.2, bf16[2688,256]{1,0:T(8,128)(2,1)S(1)} %copy-done.4), kind=kOutput, calls=%fused_computation.11 | convolution fusion | flops 2119434240 | bytes 8454144 | tf_op jit(solution)/shard_map/dot_general | solution.py:56
  268.2 4.8 %gather_fusion = f32[8,8,64,128]{3,2,1,0:T(8,128)} fusion(f32[24,8,64,128]{3,2,1,0:T(8,128)} %bitcast.46, s32[1024]{0:T(1024)S(1)} %pad_clamp_fusion.2), kind=kCustom, calls=%fused_computation | custom fusion | bytes 4194336 | tf_op jit(solution)/shard_map/gather | solution.py:26
  273.0 2.2 pad_maximum_fusion
  275.2 4.4 %copy.36 = f32[8,1,8,64,131]{4,2,0,1,3:T(8,128)} copy(f32[8,1,8,64,131]{4,3,2,0,1:T(8,128)S(1)} %pad_maximum_fusion) | data formatting | bytes 4292608 | tf_op jit(solution)/shard_map/concatenate | solution.py:26
  279.6 4.9 %all-to-all-start.1 = ((f32[8,1,8,64,131]{4,2,0,1,3:T(8,128)}), f32[8,1,8,64,131]{4,2,0,1,3:T(8,128)}, u32[]{:S(2)}, u32[]{:S(2)}) async-start(f32[8,1,8,64,131]{4,2,0,1,3:T(8,128)} %copy.36), calls=%async_computation.3 | async-start | bytes 8388608 | tf_op jit(solution)/shard_map/all_to_all | solution.py:27
  286.0 50.8 %all-to-all-done.1 = f32[8,1,8,64,131]{4,2,0,1,3:T(8,128)} async-done(((f32[8,1,8,64,131]{4,2,0,1,3:T(8,128)}), f32[8,1,8,64,131]{4,2,0,1,3:T(8,128)}, u32[]{:S(2)}, u32[]{:S(2)}) %all-to-all-start.1) | async-done | bytes 2146336 | tf_op jit(solution)/shard_map/all_to_all | solution.py:27
  336.8 4.6 %copy.43 = f32[8,1,8,64,131]{4,3,2,0,1:T(8,128)S(1)} copy(f32[8,1,8,64,131]{4,2,0,1,3:T(8,128)} %all-to-all-done.1) | data formatting | bytes 4292608 | tf_op jit(solution)/shard_map/all_to_all | solution.py:27
  341.4 2.6 copy.38
  344.0 4.2 %gather_fusion.4 = f32[32,8,8,131]{3,2,1,0:T(8,128)} fusion(f32[64,8,8,131]{3,2,1,0:T(8,128)} %bitcast.40, s32[1024]{0:T(1024)S(1)} %pad_clamp_fusion), kind=kCustom, calls=%fused_computation.4 | custom fusion | bytes 2146432 | tf_op jit(solution)/shard_map/gather | solution.py:30
  348.2 3.8 all-to-all-start.2
  352.0 1.6 fusion.17
  354.6 24.8 %all-to-all-done.2 = f32[32,1,8,8,131]{4,3,2,1,0:T(8,128)S(1)} async-done(((f32[32,1,8,8,131]{4,3,2,1,0:T(8,128)}), f32[32,1,8,8,131]{4,3,2,1,0:T(8,128)S(1)}, u32[]{:S(2)}, u32[]{:S(2)}) %all-to-all-start.2) | async-done | bytes 1073184 | tf_op jit(solution)/shard_map/all_to_all | solution.py:31
  380.7 1.5 copy.41
  382.2 1.6 fusion.9
  (42 shorter events, 7.1 us)
Async XLA Ops:
  7.2 259.7 %copy-start = (f32[24,1,8,64,3]{3,2,4,1,0:T(8,128)S(1)}, f32[24,1,8,64,3]{3,2,4,1,0:T(8,128)}, u32[]{:S(2)}) copy-start(f32[24,1,8,64,3]{3,2,4,1,0:T(8,128)} %param.11) | copy-start | bytes 442372
  7.2 150.3 %reduce-scatter.3.cloned.1.call-start = ((), (), s32[]{:S(2)}) async-start(), calls=%async_computation.5 | async-start | bytes 9289728 | tf_op jit(solution)/shard_map/reduce_scatter | solution.py:47
  7.2 47.2 %collective-permute-start.1 = (bf16[256,2688]{1,0:T(8,128)(2,1)}, bf16[256,2688]{1,0:T(8,128)(2,1)S(1)}, u32[]{:S(2)}, u32[]{:S(2)}) collective-permute-start(bf16[256,2688]{1,0:T(8,128)(2,1)} %param.8), channel_id=1, source_target_pairs={{0,16},{16,0},{1,17},{17,1},{2,18},{18,2},{3,19},{19,3},{4,20},{20... | collective-permute-start | bytes 4128776 | tf_op jit(solution)/shard_map/ppermute | solution.py:46
  10.4 30.1 %collective-permute-start = (bf16[96,256]{1,0:T(8,128)(2,1)S(1)}, bf16[96,256]{1,0:T(8,128)(2,1)S(1)}, u32[]{:S(2)}, u32[]{:S(2)}) collective-permute-start(bf16[96,256]{1,0:T(8,128)(2,1)S(1)} %get-tuple-element.29), channel_id=1, source_target_pairs={{0,16},{16,0},{1,17},{17,1},{2,18},{18,2},{3,19},{19,3},{4,20},{20... | collective-permute-start | bytes 147464 | tf_op jit(solution)/shard_map/ppermute | solution.py:43
  161.0 4.7 %copy-start.4 = (bf16[2688,256]{1,0:T(8,128)(2,1)S(1)}, bf16[2688,256]{1,0:T(8,128)(2,1)}, u32[]{:S(2)}) copy-start(bf16[2688,256]{1,0:T(8,128)(2,1)} %param.9) | copy-start | bytes 4128772
  161.0 99.7 %all-to-all-start = ((bf16[8,96,2688]{2,1,0:T(8,128)(2,1)}), bf16[8,96,2688]{2,1,0:T(8,128)(2,1)}, u32[]{:S(2)}, u32[]{:S(2)}) async-start(bf16[8,96,2688]{2,1,0:T(8,128)(2,1)} %stack.2), calls=%async_computation.1 | async-start | bytes 8257536 | tf_op jit(solution)/shard_map/all_to_all | solution.py:53
  165.7 186.3 %reduce-scatter.5.cloned.1.call-start = ((), (), s32[]{:S(2)}) async-start(), calls=%async_computation.6 | async-start | bytes 1769472 | tf_op jit(solution)/shard_map/reduce_scatter | solution.py:57
  165.8 32.0 %collective-permute-start.2 = (bf16[2688,256]{1,0:T(8,128)(2,1)S(1)}, bf16[2688,256]{1,0:T(8,128)(2,1)S(1)}, u32[]{:S(2)}, u32[]{:S(2)}) collective-permute-start(bf16[2688,256]{1,0:T(8,128)(2,1)S(1)} %copy-done.4), channel_id=1, source_target_pairs={{0,16},{16,0},{1,17},{17,1},{2,18},{18,2},{3,19},{19,3},{4,20},{20... | collective-permute-start | bytes 4128776 | tf_op jit(solution)/shard_map/ppermute | solution.py:55
  260.8 5.8 %copy-start.3 = (s32[32]{0:T(128)S(1)}, s32[32]{0:T(128)}, u32[]{:S(2)}) copy-start(s32[32]{0:T(128)} %param.12) | copy-start | bytes 388
  279.6 4.9 %copy-start.5 = (s32[32]{0:T(128)S(1)}, s32[32]{0:T(128)}, u32[]{:S(2)}) copy-start(s32[32]{0:T(128)} %param.13) | copy-start | bytes 388
  279.6 57.2 %all-to-all-start.1 = ((f32[8,1,8,64,131]{4,2,0,1,3:T(8,128)}), f32[8,1,8,64,131]{4,2,0,1,3:T(8,128)}, u32[]{:S(2)}, u32[]{:S(2)}) async-start(f32[8,1,8,64,131]{4,2,0,1,3:T(8,128)} %copy.36), calls=%async_computation.3 | async-start | bytes 8388608 | tf_op jit(solution)/shard_map/all_to_all | solution.py:27
  348.2 31.2 %all-to-all-start.2 = ((f32[32,1,8,8,131]{4,3,2,1,0:T(8,128)}), f32[32,1,8,8,131]{4,3,2,1,0:T(8,128)S(1)}, u32[]{:S(2)}, u32[]{:S(2)}) async-start(f32[32,1,8,8,131]{4,3,2,1,0:T(8,128)} %bitcast.43), calls=%async_computation.4 | async-start | bytes 4194304 | tf_op jit(solution)/shard_map/all_to_all | solution.py:31
  353.6 28.6 %collective-permute-start.3 = (f32[96,256]{1,0:T(8,128)}, f32[96,256]{1,0:T(8,128)}, u32[]{:S(2)}, u32[]{:S(2)}) collective-permute-start(f32[96,256]{1,0:T(8,128)} %get-tuple-element.27), channel_id=1, source_target_pairs={{0,16},{16,0},{1,17},{17,1},{2,18},{18,2},{3,19},{19,3},{4,20},{20... | collective-permute-start | bytes 294920 | tf_op jit(solution)/shard_map/ppermute | solution.py:59
  379.5 2.8 copy-start.1
  379.6 2.7 copy-start.2
Sparse Core Ops, SparseCore 0:
  61.5 95.9 reduce-scatter.2
  266.7 39.3 reduce-scatter.4
